TPU v7x, 512 devices: a whole 4x8x8 slice. The times are simulated.
512 devices in a mesh: section: 16 (over x_hi, y), dp: 8 (over z), mp: 4 (over x_lo, core).
Axes of the slice: x: 4 (x_hi: 2, x_lo: 2; x = x_hi * 2 + x_lo), y: 8, z: 8, core: 2. Of those that a mesh axis runs over, the one named last changes fastest.
Arguments:
- cotangent: bfloat16 [1024, 4096], P('dp', 'mp'), may hold values from -6 to 6
- saved_inputs: bfloat16 [16, 1024, 4096], P('section', 'dp', 'mp'), may hold values from -6 to 6
- pre_acts: bfloat16 [16, 1024, 4096], P('section', 'dp', 'mp'), may hold values from -8 to 8
- weights: bfloat16 [16, 4096, 4096], P('section', 'mp', 'dp'), may hold values from -0.046875 to 0.046875
- proj_in: bfloat16 [16, 4096, 64], P('section', 'mp'), may hold values from -0.09375 to 0.09375
- proj_out: bfloat16 [16, 4096, 64], P('section', 'mp'), may hold values from -0.09375 to 0.09375
- query_panels: float32 [16, 16, 4096], P('section', 'dp', 'mp'), may hold values from -4 to 4
- partners: int32 [8, 8], replicated, may hold values from 0 to 7, as said below
Outputs:
- train_panels: float32 [16, 32, 4096], P('section', 'dp', 'mp')
- scores: float32 [16, 8, 4], replicated
Inputs may be any that keep to these rules, and one draw needn't show every extreme that they name: The plan has 8 rounds: one round pairs every dp index with itself, and the others are the rounds of one round-robin plan of the 8 indices. The rows of partners hold each of these rounds once, in some order, so partners[r, partners[r, i]] = i.
All inputs are finite; a program needn't handle non-finite values.
Results may differ from a plain program's by a relative error of at most 0.02.
Values may be sent and summed in bfloat16 or wider, within the bound.
No kernel may reach another device: no remote copies, remote signals or barrier semaphores. Data moves between devices by JAX's collectives and lax.ppermute only.
A program may use at most 64 MiB of HBM per device.

v0:
```python
import math
import jax
import jax.numpy as jnp
from jax import lax
from jax.sharding import PartitionSpec as P

LEN = 32


def from_behind(block, axis, distance):
    devices = range(lax.axis_size(axis))
    route = [(i - distance, i) for i in devices if i - distance in devices]
    return lax.ppermute(block, axis, route)


def silu_slope(pre_state):
    sigma = jax.nn.sigmoid(pre_state)
    return sigma * (1.0 + pre_state * (1.0 - sigma))


def score_pair(query_rows, train_rows):
    return jnp.dot(query_rows, train_rows.T, precision=lax.Precision.HIGHEST)


def place_block(score_table, block, row_at, col_at):
    return lax.dynamic_update_slice(
        score_table,
        block[None, None],
        (jnp.asarray(row_at, jnp.int32), jnp.int32(col_at), jnp.int32(0), jnp.int32(0)),
    )


def body(cotangent, saved_inputs, pre_acts, weights, proj_in, proj_out, query_panels, partners):
    section_count = lax.axis_size("section")
    model_count = lax.axis_size("mp")
    data_count = lax.axis_size("dp")
    section_index = lax.axis_index("section")
    model_index = lax.axis_index("mp")
    data_index = lax.axis_index("dp")
    inputs = saved_inputs[0]
    pre_state = pre_acts[0]
    columns = inputs.shape[1]
    length = LEN
    examples = inputs.shape[0] // length
    low_rank = proj_in.shape[2]
    w_rows = lax.all_gather(weights[0], "dp", axis=1, tiled=True)
    step_count = examples + section_count - 1
    top_section = section_count - 1

    def advance(turn, carry):
        outgoing, stored, side_store = carry
        received = from_behind(outgoing, "section", -1)
        example_at = turn - (top_section - section_index)
        active = jnp.logical_and(example_at >= 0, example_at < examples)
        row_start = jnp.clip(example_at, 0, examples - 1) * length
        top_grad = lax.dynamic_slice_in_dim(cotangent, row_start, length, 0)
        delta_piece = jnp.where(section_index == top_section, top_grad, received)
        slopes = silu_slope(
            lax.dynamic_slice_in_dim(pre_state, row_start, length, 0).astype(jnp.float32)
        )
        grad_piece = (delta_piece.astype(jnp.float32) * slopes).astype(jnp.bfloat16)
        grad_full = lax.all_gather(grad_piece, "mp", axis=1, tiled=True)

        def through():
            back_term = lax.dot_general(
                grad_full, w_rows, (((1,), (1,)), ((), ())), preferred_element_type=jnp.float32
            )
            return (delta_piece.astype(jnp.float32) + back_term).astype(jnp.bfloat16)

        def skipped():
            return jnp.zeros_like(delta_piece)

        passed = lax.cond(active, through, skipped)
        previous = lax.dynamic_slice_in_dim(stored, row_start, length, 0)
        stored = lax.dynamic_update_slice_in_dim(
            stored, jnp.where(active, grad_piece, previous), row_start, 0
        )
        return (passed, stored, side_store)

    initial = (
        jnp.zeros((length, columns), jnp.bfloat16),
        jnp.zeros((inputs.shape[0], columns), jnp.bfloat16),
        jnp.zeros((inputs.shape[0], low_rank), jnp.float32),
    )
    final_state = lax.fori_loop(0, step_count, advance, initial)
    stored = final_state[1]
    side_store = final_state[2]
    in_part = jnp.dot(inputs, proj_in[0], preferred_element_type=jnp.float32)
    out_part = jnp.dot(stored, proj_out[0], preferred_element_type=jnp.float32)
    in_side, out_side = (
        lax.psum(in_part.astype(jnp.bfloat16), "mp").astype(jnp.float32),
        lax.psum(out_part.astype(jnp.bfloat16), "mp").astype(jnp.float32),
    )
    piece_rank = low_rank // model_count
    in_rows = lax.dynamic_slice_in_dim(in_side, model_index * piece_rank, piece_rank, 1)
    panels_here = jnp.einsum(
        "etr,etc->erc",
        in_rows.reshape(examples, length, piece_rank),
        out_side.reshape(examples, length, low_rank),
        precision=lax.Precision.HIGHEST,
    ) / math.sqrt(length)
    panels_here = panels_here.reshape(examples, piece_rank * low_rank)
    queries = query_panels[0]
    asked = queries.shape[0]
    rounds = partners.shape[0]
    score_scale = 1.0 / (low_rank * math.sqrt(section_count))
    score_table = jnp.zeros((data_count, rounds, asked, examples), jnp.float32)
    everyone = lax.all_gather(panels_here, "dp", axis=0, tiled=True).reshape(
        data_count, examples, -1
    )
    for round_at in range(rounds):
        partner = partners[round_at, data_index]
        chosen = lax.dynamic_index_in_dim(everyone, partner, 0, keepdims=False)
        score_table = place_block(score_table, score_pair(queries, chosen), data_index, round_at)
    summed = lax.psum(score_table * score_scale, ("section", "dp", "mp"))
    scores = summed.transpose(0, 2, 1, 3).reshape(data_count * asked, rounds, examples)
    return (panels_here[None], scores)


def solution(mesh):
    placed = (
        P("dp", "mp"),
        P("section", "dp", "mp"),
        P("section", "dp", "mp"),
        P("section", "mp", "dp"),
        P("section", "mp", None),
        P("section", "mp", None),
        P("section", "dp", "mp"),
        P(),
    )
    return jax.shard_map(
        body, mesh=mesh, in_specs=placed, out_specs=(P("section", "dp", "mp"), P()), check_vma=False
    )
```

profile of v0, /device:TPU:1, one launch (start us, length us, event | category | flops | bytes accessed | tf_op | source)
XLA Modules:
  0.0 635.7 jit_solution(11931362347134518088)
XLA Ops:
  25.3 87.9 %all-gather.4.cloned.1.call-done = bf16[1,1024,4096]{2,1,0:T(8,128)(2,1)} async-done(((bf16[1,1024,512]{2,1,0:T(8,128)(2,1)}), bf16[1,1024,4096]{2,1,0:T(8,128)(2,1)}) %all-gather.4.cloned.1.call-update) | async-done | bytes 8388624 | tf_op jit(solution)/shard_map/all_gather | solution.py:46
  113.8 380.4 %while.17 = (s32[]{:T(128)}, bf16[32,1024]{1,0:T(8,128)(2,1)}, bf16[128,1024]{1,0:T(8,128)(2,1)S(1)}, s32[]{:T(128)}, pred[]{:T(512)}, /*index=5*/bf16[128,1024]...) while((s32[]{:T(128)}, bf16[32,1024]{1,0:T(8,128)(2,1)}, ...), condition=%wide.region_4.5_spmd, body=%wide.region_1.4_spmd.sunk | while | flops 268959744 | bytes 9830719 | solution.py:85
  120.2 7.4 %all_gather.18 = bf16[32,4096]{1,0:T(8,128)(2,1)S(1)} all-gather(bf16[32,1024]{1,0:T(8,128)(2,1)S(1)} %get-tuple-element.282), channel_id=1, replica_groups=mesh['section'=16,'dp'=8,'mp'=4] {'mp'}, dimensions={1}, use_global_device_ids=true | all-gather | bytes 327680 | tf_op jit(solution)/shard_map/while/body/eval_jaxpr/all_gather | solution.py:62
  134.8 6.6 %all_gather.18 = bf16[32,4096]{1,0:T(8,128)(2,1)S(1)} all-gather(bf16[32,1024]{1,0:T(8,128)(2,1)S(1)} %get-tuple-element.282), channel_id=1, replica_groups=mesh['section'=16,'dp'=8,'mp'=4] {'mp'}, dimensions={1}, use_global_device_ids=true | all-gather | bytes 327680 | tf_op jit(solution)/shard_map/while/body/eval_jaxpr/all_gather | solution.py:62
  148.7 6.6 %all_gather.18 = bf16[32,4096]{1,0:T(8,128)(2,1)S(1)} all-gather(bf16[32,1024]{1,0:T(8,128)(2,1)S(1)} %get-tuple-element.282), channel_id=1, replica_groups=mesh['section'=16,'dp'=8,'mp'=4] {'mp'}, dimensions={1}, use_global_device_ids=true | all-gather | bytes 327680 | tf_op jit(solution)/shard_map/while/body/eval_jaxpr/all_gather | solution.py:62
  163.2 6.4 %all_gather.18 = bf16[32,4096]{1,0:T(8,128)(2,1)S(1)} all-gather(bf16[32,1024]{1,0:T(8,128)(2,1)S(1)} %get-tuple-element.282), channel_id=1, replica_groups=mesh['section'=16,'dp'=8,'mp'=4] {'mp'}, dimensions={1}, use_global_device_ids=true | all-gather | bytes 327680 | tf_op jit(solution)/shard_map/while/body/eval_jaxpr/all_gather | solution.py:62
  193.2 6.4 %all_gather.18 = bf16[32,4096]{1,0:T(8,128)(2,1)S(1)} all-gather(bf16[32,1024]{1,0:T(8,128)(2,1)S(1)} %get-tuple-element.282), channel_id=1, replica_groups=mesh['section'=16,'dp'=8,'mp'=4] {'mp'}, dimensions={1}, use_global_device_ids=true | all-gather | bytes 327680 | tf_op jit(solution)/shard_map/while/body/eval_jaxpr/all_gather | solution.py:62
  208.2 6.4 %all_gather.18 = bf16[32,4096]{1,0:T(8,128)(2,1)S(1)} all-gather(bf16[32,1024]{1,0:T(8,128)(2,1)S(1)} %get-tuple-element.282), channel_id=1, replica_groups=mesh['section'=16,'dp'=8,'mp'=4] {'mp'}, dimensions={1}, use_global_device_ids=true | all-gather | bytes 327680 | tf_op jit(solution)/shard_map/while/body/eval_jaxpr/all_gather | solution.py:62
  223.2 6.4 %all_gather.18 = bf16[32,4096]{1,0:T(8,128)(2,1)S(1)} all-gather(bf16[32,1024]{1,0:T(8,128)(2,1)S(1)} %get-tuple-element.282), channel_id=1, replica_groups=mesh['section'=16,'dp'=8,'mp'=4] {'mp'}, dimensions={1}, use_global_device_ids=true | all-gather | bytes 327680 | tf_op jit(solution)/shard_map/while/body/eval_jaxpr/all_gather | solution.py:62
  238.3 6.4 %all_gather.18 = bf16[32,4096]{1,0:T(8,128)(2,1)S(1)} all-gather(bf16[32,1024]{1,0:T(8,128)(2,1)S(1)} %get-tuple-element.282), channel_id=1, replica_groups=mesh['section'=16,'dp'=8,'mp'=4] {'mp'}, dimensions={1}, use_global_device_ids=true | all-gather | bytes 327680 | tf_op jit(solution)/shard_map/while/body/eval_jaxpr/all_gather | solution.py:62
  253.3 6.4 %all_gather.18 = bf16[32,4096]{1,0:T(8,128)(2,1)S(1)} all-gather(bf16[32,1024]{1,0:T(8,128)(2,1)S(1)} %get-tuple-element.282), channel_id=1, replica_groups=mesh['section'=16,'dp'=8,'mp'=4] {'mp'}, dimensions={1}, use_global_device_ids=true | all-gather | bytes 327680 | tf_op jit(solution)/shard_map/while/body/eval_jaxpr/all_gather | solution.py:62
  261.6 8.1 %collective-permute-done = bf16[32,1024]{1,0:T(8,128)(2,1)S(1)} collective-permute-done((bf16[32,1024]{1,0:T(8,128)(2,1)}, bf16[32,1024]{1,0:T(8,128)(2,1)S(1)}, u32[]{:S(2)}, u32[]{:S(2)}) %collective-permute-start) | collective-permute-done | bytes 65568 | tf_op jit(solution)/shard_map/while/body/eval_jaxpr/ppermute | solution.py:13
  270.6 6.4 %all_gather.18 = bf16[32,4096]{1,0:T(8,128)(2,1)S(1)} all-gather(bf16[32,1024]{1,0:T(8,128)(2,1)S(1)} %get-tuple-element.282), channel_id=1, replica_groups=mesh['section'=16,'dp'=8,'mp'=4] {'mp'}, dimensions={1}, use_global_device_ids=true | all-gather | bytes 327680 | tf_op jit(solution)/shard_map/while/body/eval_jaxpr/all_gather | solution.py:62
  278.9 8.2 %collective-permute-done = bf16[32,1024]{1,0:T(8,128)(2,1)S(1)} collective-permute-done((bf16[32,1024]{1,0:T(8,128)(2,1)}, bf16[32,1024]{1,0:T(8,128)(2,1)S(1)}, u32[]{:S(2)}, u32[]{:S(2)}) %collective-permute-start) | collective-permute-done | bytes 65568 | tf_op jit(solution)/shard_map/while/body/eval_jaxpr/ppermute | solution.py:13
  296.3 8.2 %collective-permute-done = bf16[32,1024]{1,0:T(8,128)(2,1)S(1)} collective-permute-done((bf16[32,1024]{1,0:T(8,128)(2,1)}, bf16[32,1024]{1,0:T(8,128)(2,1)S(1)}, u32[]{:S(2)}, u32[]{:S(2)}) %collective-permute-start) | collective-permute-done | bytes 65568 | tf_op jit(solution)/shard_map/while/body/eval_jaxpr/ppermute | solution.py:13
  313.8 8.2 %collective-permute-done = bf16[32,1024]{1,0:T(8,128)(2,1)S(1)} collective-permute-done((bf16[32,1024]{1,0:T(8,128)(2,1)}, bf16[32,1024]{1,0:T(8,128)(2,1)S(1)}, u32[]{:S(2)}, u32[]{:S(2)}) %collective-permute-start) | collective-permute-done | bytes 65568 | tf_op jit(solution)/shard_map/while/body/eval_jaxpr/ppermute | solution.py:13
  331.2 8.2 %collective-permute-done = bf16[32,1024]{1,0:T(8,128)(2,1)S(1)} collective-permute-done((bf16[32,1024]{1,0:T(8,128)(2,1)}, bf16[32,1024]{1,0:T(8,128)(2,1)S(1)}, u32[]{:S(2)}, u32[]{:S(2)}) %collective-permute-start) | collective-permute-done | bytes 65568 | tf_op jit(solution)/shard_map/while/body/eval_jaxpr/ppermute | solution.py:13
  348.6 61.6 %collective-permute-done = bf16[32,1024]{1,0:T(8,128)(2,1)S(1)} collective-permute-done((bf16[32,1024]{1,0:T(8,128)(2,1)}, bf16[32,1024]{1,0:T(8,128)(2,1)S(1)}, u32[]{:S(2)}, u32[]{:S(2)}) %collective-permute-start) | collective-permute-done | bytes 65568 | tf_op jit(solution)/shard_map/while/body/eval_jaxpr/ppermute | solution.py:13
  417.5 6.6 %conditional.2 = (bf16[32,1024]{1,0:T(8,128)(2,1)}) conditional(s32[]{:T(128)} %convert_element_type.80, () %tuple.60, (bf16[32,1024]{1,0:T(8,128)(2,1)S(1)}, bf16[32,4096]{1,0:T(8,128)(2,1)S(1)}, bf16[1024,4096]{1,0:T(8,128)(2,1)}) %tuple.61), branch_computations={%region_2.2_spmd, %region_3.3_spmd} | conditional | flops 268533760 | bytes 8781832 | solution.py:73
  417.5 6.6 %fusion = bf16[32,1024]{1,0:T(8,128)(2,1)} fusion(bf16[32,4096]{1,0:T(8,128)(2,1)S(1)} %get-tuple-element.181, bf16[1024,4096]{1,0:T(8,128)(2,1)} %get-tuple-element.182, bf16[32,1024]{1,0:T(8,128)(2,1)S(1)} %get-tuple-element.180), kind=kOutput, calls=%fused_computation.1 | convolution fusion | flops 268533760 | bytes 8781824 | tf_op jit(solution)/shard_map/while/body/eval_jaxpr/cond/branch_1_fun/dot_general | solution.py:65
  425.4 8.2 %collective-permute-done = bf16[32,1024]{1,0:T(8,128)(2,1)S(1)} collective-permute-done((bf16[32,1024]{1,0:T(8,128)(2,1)}, bf16[32,1024]{1,0:T(8,128)(2,1)S(1)}, u32[]{:S(2)}, u32[]{:S(2)}) %collective-permute-start) | collective-permute-done | bytes 65568 | tf_op jit(solution)/shard_map/while/body/eval_jaxpr/ppermute | solution.py:13
  440.8 6.6 %conditional.2 = (bf16[32,1024]{1,0:T(8,128)(2,1)}) conditional(s32[]{:T(128)} %convert_element_type.80, () %tuple.60, (bf16[32,1024]{1,0:T(8,128)(2,1)S(1)}, bf16[32,4096]{1,0:T(8,128)(2,1)S(1)}, bf16[1024,4096]{1,0:T(8,128)(2,1)}) %tuple.61), branch_computations={%region_2.2_spmd, %region_3.3_spmd} | conditional | flops 268533760 | bytes 8781832 | solution.py:73
  440.8 6.6 %fusion = bf16[32,1024]{1,0:T(8,128)(2,1)} fusion(bf16[32,4096]{1,0:T(8,128)(2,1)S(1)} %get-tuple-element.181, bf16[1024,4096]{1,0:T(8,128)(2,1)} %get-tuple-element.182, bf16[32,1024]{1,0:T(8,128)(2,1)S(1)} %get-tuple-element.180), kind=kOutput, calls=%fused_computation.1 | convolution fusion | flops 268533760 | bytes 8781824 | tf_op jit(solution)/shard_map/while/body/eval_jaxpr/cond/branch_1_fun/dot_general | solution.py:65
  448.7 8.3 %collective-permute-done = bf16[32,1024]{1,0:T(8,128)(2,1)S(1)} collective-permute-done((bf16[32,1024]{1,0:T(8,128)(2,1)}, bf16[32,1024]{1,0:T(8,128)(2,1)S(1)}, u32[]{:S(2)}, u32[]{:S(2)}) %collective-permute-start) | collective-permute-done | bytes 65568 | tf_op jit(solution)/shard_map/while/body/eval_jaxpr/ppermute | solution.py:13
  464.3 6.6 %conditional.2 = (bf16[32,1024]{1,0:T(8,128)(2,1)}) conditional(s32[]{:T(128)} %convert_element_type.80, () %tuple.60, (bf16[32,1024]{1,0:T(8,128)(2,1)S(1)}, bf16[32,4096]{1,0:T(8,128)(2,1)S(1)}, bf16[1024,4096]{1,0:T(8,128)(2,1)}) %tuple.61), branch_computations={%region_2.2_spmd, %region_3.3_spmd} | conditional | flops 268533760 | bytes 8781832 | solution.py:73
  464.3 6.6 %fusion = bf16[32,1024]{1,0:T(8,128)(2,1)} fusion(bf16[32,4096]{1,0:T(8,128)(2,1)S(1)} %get-tuple-element.181, bf16[1024,4096]{1,0:T(8,128)(2,1)} %get-tuple-element.182, bf16[32,1024]{1,0:T(8,128)(2,1)S(1)} %get-tuple-element.180), kind=kOutput, calls=%fused_computation.1 | convolution fusion | flops 268533760 | bytes 8781824 | tf_op jit(solution)/shard_map/while/body/eval_jaxpr/cond/branch_1_fun/dot_general | solution.py:65
  472.2 8.2 %collective-permute-done = bf16[32,1024]{1,0:T(8,128)(2,1)S(1)} collective-permute-done((bf16[32,1024]{1,0:T(8,128)(2,1)}, bf16[32,1024]{1,0:T(8,128)(2,1)S(1)}, u32[]{:S(2)}, u32[]{:S(2)}) %collective-permute-start) | collective-permute-done | bytes 65568 | tf_op jit(solution)/shard_map/while/body/eval_jaxpr/ppermute | solution.py:13
  487.7 6.6 %conditional.2 = (bf16[32,1024]{1,0:T(8,128)(2,1)}) conditional(s32[]{:T(128)} %convert_element_type.80, () %tuple.60, (bf16[32,1024]{1,0:T(8,128)(2,1)S(1)}, bf16[32,4096]{1,0:T(8,128)(2,1)S(1)}, bf16[1024,4096]{1,0:T(8,128)(2,1)}) %tuple.61), branch_computations={%region_2.2_spmd, %region_3.3_spmd} | conditional | flops 268533760 | bytes 8781832 | solution.py:73
  487.7 6.6 %fusion = bf16[32,1024]{1,0:T(8,128)(2,1)} fusion(bf16[32,4096]{1,0:T(8,128)(2,1)S(1)} %get-tuple-element.181, bf16[1024,4096]{1,0:T(8,128)(2,1)} %get-tuple-element.182, bf16[32,1024]{1,0:T(8,128)(2,1)S(1)} %get-tuple-element.180), kind=kOutput, calls=%fused_computation.1 | convolution fusion | flops 268533760 | bytes 8781824 | tf_op jit(solution)/shard_map/while/body/eval_jaxpr/cond/branch_1_fun/dot_general | solution.py:65
  494.6 10.8 %all-reduce = (bf16[4,32,64]{2,1,0:T(8,128)(2,1)S(1)}, bf16[128,64]{0,1:T(8,128)(2,1)S(1)}) all-reduce(bf16[4,32,64]{2,1,0:T(8,128)(2,1)S(1)} %bitcast.104, bf16[128,64]{0,1:T(8,128)(2,1)S(1)} %convolution_convert_fusion.1), channel_id=1, replica_groups=mesh['section'=16,'dp'=8,'mp'=4] {'mp'}, use_global_device_ids=true, to_apply=%region_5.6 | all-reduce | flops 16384 | bytes 65536 | tf_op jit(solution)/shard_map/psum | solution.py:92
  505.7 18.5 %all-gather.1 = f32[8,4,1024]{2,1,0:T(4,128)S(1)} all-gather(f32[1,4,1024]{2,1,0:T(4,128)S(1)} %broadcast_in_dim_reshape.3), channel_id=1, replica_groups=mesh['section'=16,'dp'=8,'mp'=4] {'dp'}, dimensions={0}, use_global_device_ids=true | all-gather | bytes 147456 | tf_op jit(solution)/shard_map/all_gather | solution.py:108
  529.0 99.2 %psum.23 = f32[16,8,4]{1,0,2:T(8,128)S(1)} all-reduce(f32[16,8,4]{1,0,2:T(8,128)S(1)} %bitcast.105), channel_id=1, replica_groups=mesh['section'=16,'dp'=8,'mp'=4] {'section','dp','mp'}, use_global_device_ids=true, to_apply=%region_6.7 | all-reduce | flops 512 | bytes 4096 | tf_op jit(solution)/shard_map/psum | solution.py:115
  (134 shorter events, 180.7 us)
Async XLA Ops:
  7.2 17.0 %copy-start = (bf16[1,128,1024]{2,1,0:T(8,128)(2,1)S(1)}, bf16[1,128,1024]{2,1,0:T(8,128)(2,1)}, u32[]{:S(2)}) copy-start(bf16[1,128,1024]{2,1,0:T(8,128)(2,1)} %param.13) | copy-start | bytes 786436
  7.2 106.0 %all-gather.4.cloned.1.call-start = ((), (), s32[]{:S(2)}) async-start(), calls=%async_computation | async-start | bytes 9437184 | tf_op jit(solution)/shard_map/all_gather | solution.py:46
  113.8 380.5 %copy-start.2 = (bf16[1,1024,64]{1,2,0:T(8,128)(2,1)S(1)}, bf16[1,1024,64]{1,2,0:T(8,128)(2,1)}, u32[]{:S(2)}) copy-start(bf16[1,1024,64]{1,2,0:T(8,128)(2,1)} %param.17) | copy-start | bytes 393220
  113.8 410.4 %copy-start.1 = (f32[1,2,1024]{2,1,0:T(2,128)S(1)}, f32[1,2,1024]{2,1,0:T(2,128)}, u32[]{:S(2)}) copy-start(f32[1,2,1024]{2,1,0:T(2,128)} %param.18) | copy-start | bytes 24580
  113.9 5.4 collective-permute-start
  128.2 5.6 collective-permute-start
  142.1 5.6 collective-permute-start
  155.9 6.3 collective-permute-start
  170.1 7.1 %collective-permute-start = (bf16[32,1024]{1,0:T(8,128)(2,1)}, bf16[32,1024]{1,0:T(8,128)(2,1)S(1)}, u32[]{:S(2)}, u32[]{:S(2)}) collective-permute-start(bf16[32,1024]{1,0:T(8,128)(2,1)} %get-tuple-element.299), channel_id=1, source_target_pairs={{32,0},{64,32},{96,64},{128,96},{160,128},{192,160},{224,192},{256... | collective-permute-start | bytes 196616 | tf_op jit(solution)/shard_map/while/body/eval_jaxpr/ppermute | solution.py:13
  185.2 7.1 %collective-permute-start = (bf16[32,1024]{1,0:T(8,128)(2,1)}, bf16[32,1024]{1,0:T(8,128)(2,1)S(1)}, u32[]{:S(2)}, u32[]{:S(2)}) collective-permute-start(bf16[32,1024]{1,0:T(8,128)(2,1)} %get-tuple-element.299), channel_id=1, source_target_pairs={{32,0},{64,32},{96,64},{128,96},{160,128},{192,160},{224,192},{256... | collective-permute-start | bytes 196616 | tf_op jit(solution)/shard_map/while/body/eval_jaxpr/ppermute | solution.py:13
  200.2 7.1 %collective-permute-start = (bf16[32,1024]{1,0:T(8,128)(2,1)}, bf16[32,1024]{1,0:T(8,128)(2,1)S(1)}, u32[]{:S(2)}, u32[]{:S(2)}) collective-permute-start(bf16[32,1024]{1,0:T(8,128)(2,1)} %get-tuple-element.299), channel_id=1, source_target_pairs={{32,0},{64,32},{96,64},{128,96},{160,128},{192,160},{224,192},{256... | collective-permute-start | bytes 196616 | tf_op jit(solution)/shard_map/while/body/eval_jaxpr/ppermute | solution.py:13
  215.2 7.1 %collective-permute-start = (bf16[32,1024]{1,0:T(8,128)(2,1)}, bf16[32,1024]{1,0:T(8,128)(2,1)S(1)}, u32[]{:S(2)}, u32[]{:S(2)}) collective-permute-start(bf16[32,1024]{1,0:T(8,128)(2,1)} %get-tuple-element.299), channel_id=1, source_target_pairs={{32,0},{64,32},{96,64},{128,96},{160,128},{192,160},{224,192},{256... | collective-permute-start | bytes 196616 | tf_op jit(solution)/shard_map/while/body/eval_jaxpr/ppermute | solution.py:13
  230.2 7.1 %collective-permute-start = (bf16[32,1024]{1,0:T(8,128)(2,1)}, bf16[32,1024]{1,0:T(8,128)(2,1)S(1)}, u32[]{:S(2)}, u32[]{:S(2)}) collective-permute-start(bf16[32,1024]{1,0:T(8,128)(2,1)} %get-tuple-element.299), channel_id=1, source_target_pairs={{32,0},{64,32},{96,64},{128,96},{160,128},{192,160},{224,192},{256... | collective-permute-start | bytes 196616 | tf_op jit(solution)/shard_map/while/body/eval_jaxpr/ppermute | solution.py:13
  245.3 7.1 %collective-permute-start = (bf16[32,1024]{1,0:T(8,128)(2,1)}, bf16[32,1024]{1,0:T(8,128)(2,1)S(1)}, u32[]{:S(2)}, u32[]{:S(2)}) collective-permute-start(bf16[32,1024]{1,0:T(8,128)(2,1)} %get-tuple-element.299), channel_id=1, source_target_pairs={{32,0},{64,32},{96,64},{128,96},{160,128},{192,160},{224,192},{256... | collective-permute-start | bytes 196616 | tf_op jit(solution)/shard_map/while/body/eval_jaxpr/ppermute | solution.py:13
  260.3 9.4 %collective-permute-start = (bf16[32,1024]{1,0:T(8,128)(2,1)}, bf16[32,1024]{1,0:T(8,128)(2,1)S(1)}, u32[]{:S(2)}, u32[]{:S(2)}) collective-permute-start(bf16[32,1024]{1,0:T(8,128)(2,1)} %get-tuple-element.299), channel_id=1, source_target_pairs={{32,0},{64,32},{96,64},{128,96},{160,128},{192,160},{224,192},{256... | collective-permute-start | bytes 196616 | tf_op jit(solution)/shard_map/while/body/eval_jaxpr/ppermute | solution.py:13
  277.6 9.5 %collective-permute-start = (bf16[32,1024]{1,0:T(8,128)(2,1)}, bf16[32,1024]{1,0:T(8,128)(2,1)S(1)}, u32[]{:S(2)}, u32[]{:S(2)}) collective-permute-start(bf16[32,1024]{1,0:T(8,128)(2,1)} %get-tuple-element.299), channel_id=1, source_target_pairs={{32,0},{64,32},{96,64},{128,96},{160,128},{192,160},{224,192},{256... | collective-permute-start | bytes 196616 | tf_op jit(solution)/shard_map/while/body/eval_jaxpr/ppermute | solution.py:13
  295.0 9.5 %collective-permute-start = (bf16[32,1024]{1,0:T(8,128)(2,1)}, bf16[32,1024]{1,0:T(8,128)(2,1)S(1)}, u32[]{:S(2)}, u32[]{:S(2)}) collective-permute-start(bf16[32,1024]{1,0:T(8,128)(2,1)} %get-tuple-element.299), channel_id=1, source_target_pairs={{32,0},{64,32},{96,64},{128,96},{160,128},{192,160},{224,192},{256... | collective-permute-start | bytes 196616 | tf_op jit(solution)/shard_map/while/body/eval_jaxpr/ppermute | solution.py:13
  312.4 9.5 %collective-permute-start = (bf16[32,1024]{1,0:T(8,128)(2,1)}, bf16[32,1024]{1,0:T(8,128)(2,1)S(1)}, u32[]{:S(2)}, u32[]{:S(2)}) collective-permute-start(bf16[32,1024]{1,0:T(8,128)(2,1)} %get-tuple-element.299), channel_id=1, source_target_pairs={{32,0},{64,32},{96,64},{128,96},{160,128},{192,160},{224,192},{256... | collective-permute-start | bytes 196616 | tf_op jit(solution)/shard_map/while/body/eval_jaxpr/ppermute | solution.py:13
  329.9 9.5 %collective-permute-start = (bf16[32,1024]{1,0:T(8,128)(2,1)}, bf16[32,1024]{1,0:T(8,128)(2,1)S(1)}, u32[]{:S(2)}, u32[]{:S(2)}) collective-permute-start(bf16[32,1024]{1,0:T(8,128)(2,1)} %get-tuple-element.299), channel_id=1, source_target_pairs={{32,0},{64,32},{96,64},{128,96},{160,128},{192,160},{224,192},{256... | collective-permute-start | bytes 196616 | tf_op jit(solution)/shard_map/while/body/eval_jaxpr/ppermute | solution.py:13
  347.3 62.9 %collective-permute-start = (bf16[32,1024]{1,0:T(8,128)(2,1)}, bf16[32,1024]{1,0:T(8,128)(2,1)S(1)}, u32[]{:S(2)}, u32[]{:S(2)}) collective-permute-start(bf16[32,1024]{1,0:T(8,128)(2,1)} %get-tuple-element.299), channel_id=1, source_target_pairs={{32,0},{64,32},{96,64},{128,96},{160,128},{192,160},{224,192},{256... | collective-permute-start | bytes 196616 | tf_op jit(solution)/shard_map/while/body/eval_jaxpr/ppermute | solution.py:13
  424.0 9.6 %collective-permute-start = (bf16[32,1024]{1,0:T(8,128)(2,1)}, bf16[32,1024]{1,0:T(8,128)(2,1)S(1)}, u32[]{:S(2)}, u32[]{:S(2)}) collective-permute-start(bf16[32,1024]{1,0:T(8,128)(2,1)} %get-tuple-element.299), channel_id=1, source_target_pairs={{32,0},{64,32},{96,64},{128,96},{160,128},{192,160},{224,192},{256... | collective-permute-start | bytes 196616 | tf_op jit(solution)/shard_map/while/body/eval_jaxpr/ppermute | solution.py:13
  447.4 9.6 %collective-permute-start = (bf16[32,1024]{1,0:T(8,128)(2,1)}, bf16[32,1024]{1,0:T(8,128)(2,1)S(1)}, u32[]{:S(2)}, u32[]{:S(2)}) collective-permute-start(bf16[32,1024]{1,0:T(8,128)(2,1)} %get-tuple-element.299), channel_id=1, source_target_pairs={{32,0},{64,32},{96,64},{128,96},{160,128},{192,160},{224,192},{256... | collective-permute-start | bytes 196616 | tf_op jit(solution)/shard_map/while/body/eval_jaxpr/ppermute | solution.py:13
  470.9 9.6 %collective-permute-start = (bf16[32,1024]{1,0:T(8,128)(2,1)}, bf16[32,1024]{1,0:T(8,128)(2,1)S(1)}, u32[]{:S(2)}, u32[]{:S(2)}) collective-permute-start(bf16[32,1024]{1,0:T(8,128)(2,1)} %get-tuple-element.299), channel_id=1, source_target_pairs={{32,0},{64,32},{96,64},{128,96},{160,128},{192,160},{224,192},{256... | collective-permute-start | bytes 196616 | tf_op jit(solution)/shard_map/while/body/eval_jaxpr/ppermute | solution.py:13
  505.7 123.2 %copy-start.3 = (f32[1,4,1024]{2,1,0:T(4,128)}, f32[1,4,1024]{2,1,0:T(4,128)S(1)}, u32[]{:S(2)}) copy-start(f32[1,4,1024]{2,1,0:T(4,128)S(1)} %broadcast_in_dim_reshape.3) | copy-start | bytes 49156
Sparse Core Ops, SparseCore 0:
  10.1 103.0 all-gather.3
where the time goes:
time: 638 us; the launch traced here: 636 us
  waiting for transfers between devices  268 us (42%)
  blocking collectives  251 us (39%)
  matrix products  29.3 us (5%)
  between operations  28.8 us (5%)
  starting transfers between devices  24.5 us (4%)
  other arithmetic  18.2 us (3%)
  local copies, waits for them, and re-layouts  15.9 us (2%)
    ppermute x19, waiting for transfers between devices, from_behind(): return lax.ppermute(block, axis, route)  179 us
    all_gather x19, blocking collectives, advance(): grad_full = lax.all_gather(grad_piece, 'mp', axis=1, tiled=True)  122 us
    psum x1, blocking collectives, body(): summed = lax.psum(score_table * score_scale, ('section', 'dp', 'mp'))  99.2 us
    all_gather x1, waiting for transfers between devices, body(): w_rows = lax.all_gather(weights[0], 'dp', axis=1, tiled=True)  87.9 us
    dot_general x4, matrix products, through(): lax.dot_general(grad_full, w_rows, (((1,), (1,)), ((), ())), preferred_el...  26.4 us
    ppermute x19, starting transfers between devices, from_behind(): return lax.ppermute(block, axis, route)  24.5 us
    all_gather x1, blocking collectives, body(): lax.all_gather(panels_here, 'dp', axis=0, tiled=True)  18.5 us
    dynamic_update_slice x19, other arithmetic, advance(): lax.dynamic_update_slice_in_dim(stored, jnp.where(active, grad_piece, pre...  18.2 us
  transfers between devices with their start and end apart: 20, of which 20 were waited for; matrix products, arithmetic and copies ran while one was open for 0% of the time, Pallas kernels for 0%

commit v1 on v0

--- a/solution.py
+++ b/solution.py
@@ -43,7 +43,9 @@
     length = LEN
     examples = inputs.shape[0] // length
     low_rank = proj_in.shape[2]
-    w_rows = lax.all_gather(weights[0], "dp", axis=1, tiled=True)
+    w_rows = jnp.concatenate(
+        lax.all_to_all(jnp.stack([weights[0]] * lax.axis_size("dp")), "dp", 0, 0), axis=1
+    )
     step_count = examples + section_count - 1
     top_section = section_count - 1
 

time: 638 us -> 744 us (1.17)
  waiting for transfers between devices: 268 us -> 351 us
  local copies, waits for them, and re-layouts: 15.9 us -> 42.8 us
  between operations: 28.8 us -> 15.8 us
  starting transfers between devices: 24.5 us -> 35.4 us
    all_to_all x0 -> x1, waiting for transfers between devices: none -> 171 us  [body(): lax.all_to_all(jnp.stack([weights[0]] * lax.axis_size('dp')), 'dp', 0, 0)]
    all_gather x1 -> x0, waiting for transfers between devices: 87.9 us -> none  [body(): w_rows = lax.all_gather(weights[0], 'dp', axis=1, tiled=True)]
    all_to_all x0 -> x1, local copies, waits for them, and re-layouts: none -> 11.4 us  [body(): lax.all_to_all(jnp.stack([weights[0]] * lax.axis_size('dp')), 'dp', 0, 0)]
    while x0 -> x1, local copies, waits for them, and re-layouts: none -> 11.3 us  [body(): final_state = lax.fori_loop(0, step_count, advance, initial)]
    all_to_all x0 -> x1, starting transfers between devices: none -> 11 us  [body(): lax.all_to_all(jnp.stack([weights[0]] * lax.axis_size('dp')), 'dp', 0, 0)]
    another operation x16 -> x17, local copies, waits for them, and re-layouts: 10.1 us -> 15.2 us
where the time goes in v1:
time: 744 us; the launch traced here: 742 us
  waiting for transfers between devices  351 us (47%)
  blocking collectives  250 us (34%)
  local copies, waits for them, and re-layouts  42.8 us (6%)
  starting transfers between devices  35.4 us (5%)
  matrix products  28.3 us (4%)
  other arithmetic  18.2 us (2%)
  between operations  15.8 us (2%)
    ppermute x19, waiting for transfers between devices, from_behind(): return lax.ppermute(block, axis, route)  180 us
    all_to_all x1, waiting for transfers between devices, body(): lax.all_to_all(jnp.stack([weights[0]] * lax.axis_size('dp')), 'dp', 0, 0)  171 us
    all_gather x19, blocking collectives, advance(): grad_full = lax.all_gather(grad_piece, 'mp', axis=1, tiled=True)  122 us
    psum x1, blocking collectives, body(): summed = lax.psum(score_table * score_scale, ('section', 'dp', 'mp'))  98.5 us
    dot_general x4, matrix products, through(): lax.dot_general(grad_full, w_rows, (((1,), (1,)), ((), ())), preferred_el...  26.3 us
    ppermute x19, starting transfers between devices, from_behind(): return lax.ppermute(block, axis, route)  24.5 us
    all_gather x1, blocking collectives, body(): lax.all_gather(panels_here, 'dp', axis=0, tiled=True)  18.4 us
    dynamic_update_slice x19, other arithmetic, advance(): lax.dynamic_update_slice_in_dim(stored, jnp.where(active, grad_piece, pre...  18.2 us
  transfers between devices with their start and end apart: 20, of which 20 were waited for; matrix products, arithmetic and copies ran while one was open for 0% of the time, Pallas kernels for 0%

profile of v1, /device:TPU:1, one launch (start us, length us, event | category | flops | bytes accessed | tf_op | source)
XLA Modules:
  0.0 741.7 jit_solution(6881397531740330886)
XLA Ops:
  5.9 11.0 %all-to-all-start = ((bf16[8,1024,512]{2,1,0:T(8,128)(2,1)}), bf16[8,1024,512]{2,1,0:T(8,128)(2,1)}, u32[]{:S(2)}, u32[]{:S(2)}) async-start(bf16[8,1024,512]{2,1,0:T(8,128)(2,1)} %stack.3), calls=%async_computation | async-start | bytes 16777216 | tf_op jit(solution)/shard_map/all_to_all | solution.py:47
  32.8 171.0 %all-to-all-done = bf16[8,1024,512]{2,1,0:T(8,128)(2,1)} async-done(((bf16[8,1024,512]{2,1,0:T(8,128)(2,1)}), bf16[8,1024,512]{2,1,0:T(8,128)(2,1)}, u32[]{:S(2)}, u32[]{:S(2)}) %all-to-all-start) | async-done | bytes 8388640 | tf_op jit(solution)/shard_map/all_to_all | solution.py:47
  203.8 11.4 %copy.41 = bf16[8,1024,512]{1,2,0:T(8,128)(2,1)} copy(bf16[8,1024,512]{2,1,0:T(8,128)(2,1)} %all-to-all-done) | data formatting | bytes 16777216 | tf_op jit(solution)/shard_map/all_to_all | solution.py:47
  215.2 11.3 %copy.42 = bf16[1024,4096]{1,0:T(8,128)(2,1)} copy(bf16[1024,4096]{0,1:T(8,128)(2,1)} %bitcast.105) | data formatting | bytes 16777216 | tf_op jit(solution)/shard_map/while | solution.py:87
  227.1 380.7 %while.17 = (s32[]{:T(128)}, bf16[32,1024]{1,0:T(8,128)(2,1)}, bf16[128,1024]{1,0:T(8,128)(2,1)S(1)}, s32[]{:T(128)}, pred[]{:T(512)}, /*index=5*/bf16[128,1024]...) while((s32[]{:T(128)}, bf16[32,1024]{1,0:T(8,128)(2,1)}, ...), condition=%wide.region_4.5_spmd, body=%wide.region_1.4_spmd.sunk | while | flops 268959744 | bytes 9830719 | solution.py:87
  233.4 7.3 all_gather.14
  247.9 6.6 all_gather.14
  261.7 6.6 all_gather.14
  276.5 6.4 all_gather.14
  291.5 6.4 all_gather.14
  306.5 6.4 all_gather.14
  321.5 6.4 all_gather.14
  375.1 8.2 %collective-permute-done = bf16[32,1024]{1,0:T(8,128)(2,1)S(1)} collective-permute-done((bf16[32,1024]{1,0:T(8,128)(2,1)}, bf16[32,1024]{1,0:T(8,128)(2,1)S(1)}, u32[]{:S(2)}, u32[]{:S(2)}) %collective-permute-start) | collective-permute-done | bytes 65568 | tf_op jit(solution)/shard_map/while/body/eval_jaxpr/ppermute | solution.py:13
  392.6 8.2 %collective-permute-done = bf16[32,1024]{1,0:T(8,128)(2,1)S(1)} collective-permute-done((bf16[32,1024]{1,0:T(8,128)(2,1)}, bf16[32,1024]{1,0:T(8,128)(2,1)S(1)}, u32[]{:S(2)}, u32[]{:S(2)}) %collective-permute-start) | collective-permute-done | bytes 65568 | tf_op jit(solution)/shard_map/while/body/eval_jaxpr/ppermute | solution.py:13
  410.0 8.2 %collective-permute-done = bf16[32,1024]{1,0:T(8,128)(2,1)S(1)} collective-permute-done((bf16[32,1024]{1,0:T(8,128)(2,1)}, bf16[32,1024]{1,0:T(8,128)(2,1)S(1)}, u32[]{:S(2)}, u32[]{:S(2)}) %collective-permute-start) | collective-permute-done | bytes 65568 | tf_op jit(solution)/shard_map/while/body/eval_jaxpr/ppermute | solution.py:13
  427.4 8.2 %collective-permute-done = bf16[32,1024]{1,0:T(8,128)(2,1)S(1)} collective-permute-done((bf16[32,1024]{1,0:T(8,128)(2,1)}, bf16[32,1024]{1,0:T(8,128)(2,1)S(1)}, u32[]{:S(2)}, u32[]{:S(2)}) %collective-permute-start) | collective-permute-done | bytes 65568 | tf_op jit(solution)/shard_map/while/body/eval_jaxpr/ppermute | solution.py:13
  444.8 8.2 %collective-permute-done = bf16[32,1024]{1,0:T(8,128)(2,1)S(1)} collective-permute-done((bf16[32,1024]{1,0:T(8,128)(2,1)}, bf16[32,1024]{1,0:T(8,128)(2,1)S(1)}, u32[]{:S(2)}, u32[]{:S(2)}) %collective-permute-start) | collective-permute-done | bytes 65568 | tf_op jit(solution)/shard_map/while/body/eval_jaxpr/ppermute | solution.py:13
  462.2 61.6 %collective-permute-done = bf16[32,1024]{1,0:T(8,128)(2,1)S(1)} collective-permute-done((bf16[32,1024]{1,0:T(8,128)(2,1)}, bf16[32,1024]{1,0:T(8,128)(2,1)S(1)}, u32[]{:S(2)}, u32[]{:S(2)}) %collective-permute-start) | collective-permute-done | bytes 65568 | tf_op jit(solution)/shard_map/while/body/eval_jaxpr/ppermute | solution.py:13
  531.0 6.6 conditional.2
  531.0 6.6 fusion
  538.9 8.3 %collective-permute-done = bf16[32,1024]{1,0:T(8,128)(2,1)S(1)} collective-permute-done((bf16[32,1024]{1,0:T(8,128)(2,1)}, bf16[32,1024]{1,0:T(8,128)(2,1)S(1)}, u32[]{:S(2)}, u32[]{:S(2)}) %collective-permute-start) | collective-permute-done | bytes 65568 | tf_op jit(solution)/shard_map/while/body/eval_jaxpr/ppermute | solution.py:13
  554.4 6.6 conditional.2
  554.4 6.6 fusion
  562.3 8.3 %collective-permute-done = bf16[32,1024]{1,0:T(8,128)(2,1)S(1)} collective-permute-done((bf16[32,1024]{1,0:T(8,128)(2,1)}, bf16[32,1024]{1,0:T(8,128)(2,1)S(1)}, u32[]{:S(2)}, u32[]{:S(2)}) %collective-permute-start) | collective-permute-done | bytes 65568 | tf_op jit(solution)/shard_map/while/body/eval_jaxpr/ppermute | solution.py:13
  577.9 6.6 conditional.2
  577.9 6.6 fusion
  585.8 8.3 %collective-permute-done = bf16[32,1024]{1,0:T(8,128)(2,1)S(1)} collective-permute-done((bf16[32,1024]{1,0:T(8,128)(2,1)}, bf16[32,1024]{1,0:T(8,128)(2,1)S(1)}, u32[]{:S(2)}, u32[]{:S(2)}) %collective-permute-start) | collective-permute-done | bytes 65568 | tf_op jit(solution)/shard_map/while/body/eval_jaxpr/ppermute | solution.py:13
  601.2 6.6 conditional.2
  601.2 6.6 fusion
  608.2 10.8 %all-reduce = (bf16[4,32,64]{2,1,0:T(8,128)(2,1)S(1)}, bf16[128,64]{0,1:T(8,128)(2,1)S(1)}) all-reduce(bf16[4,32,64]{2,1,0:T(8,128)(2,1)S(1)} %bitcast.108, bf16[128,64]{0,1:T(8,128)(2,1)S(1)} %convolution_convert_fusion.1), channel_id=1, replica_groups=mesh['section'=16,'dp'=8,'mp'=4] {'mp'}, use_global_device_ids=true, to_apply=%region_5.6 | all-reduce | flops 16384 | bytes 65536 | tf_op jit(solution)/shard_map/psum | solution.py:94
  619.3 18.4 %all-gather = f32[8,4,1024]{2,1,0:T(4,128)S(1)} all-gather(f32[1,4,1024]{2,1,0:T(4,128)S(1)} %broadcast_in_dim_reshape.3), channel_id=1, replica_groups=mesh['section'=16,'dp'=8,'mp'=4] {'dp'}, dimensions={0}, use_global_device_ids=true | all-gather | bytes 147456 | tf_op jit(solution)/shard_map/all_gather | solution.py:110
  642.5 98.5 %psum.23 = f32[16,8,4]{1,0,2:T(8,128)S(1)} all-reduce(f32[16,8,4]{1,0,2:T(8,128)S(1)} %bitcast.109), channel_id=1, replica_groups=mesh['section'=16,'dp'=8,'mp'=4] {'section','dp','mp'}, use_global_device_ids=true, to_apply=%region_6.7 | all-reduce | flops 512 | bytes 4096 | tf_op jit(solution)/shard_map/psum | solution.py:117
  (140 shorter events, 202.8 us)
Async XLA Ops:
  0.6 31.9 %copy-start = (bf16[1,128,1024]{2,1,0:T(8,128)(2,1)S(1)}, bf16[1,128,1024]{2,1,0:T(8,128)(2,1)}, u32[]{:S(2)}) copy-start(bf16[1,128,1024]{2,1,0:T(8,128)(2,1)} %param.13) | copy-start | bytes 786436
  5.9 11.0 %copy-start.5 = (s32[8,8]{1,0:T(8,128)S(1)}, s32[8,8]{1,0:T(8,128)}, u32[]{:S(2)}) copy-start(s32[8,8]{1,0:T(8,128)} %param.19) | copy-start | bytes 772
  5.9 26.7 %copy-start.2 = (bf16[1,1024,64]{1,2,0:T(8,128)(2,1)S(1)}, bf16[1,1024,64]{1,2,0:T(8,128)(2,1)}, u32[]{:S(2)}) copy-start(bf16[1,1024,64]{1,2,0:T(8,128)(2,1)} %param.16) | copy-start | bytes 393220
  5.9 197.9 %all-to-all-start = ((bf16[8,1024,512]{2,1,0:T(8,128)(2,1)}), bf16[8,1024,512]{2,1,0:T(8,128)(2,1)}, u32[]{:S(2)}, u32[]{:S(2)}) async-start(bf16[8,1024,512]{2,1,0:T(8,128)(2,1)} %stack.3), calls=%async_computation | async-start | bytes 16777216 | tf_op jit(solution)/shard_map/all_to_all | solution.py:47
  227.1 380.7 %copy-start.3 = (bf16[1,1024,64]{1,2,0:T(8,128)(2,1)S(1)}, bf16[1,1024,64]{1,2,0:T(8,128)(2,1)}, u32[]{:S(2)}) copy-start(bf16[1,1024,64]{1,2,0:T(8,128)(2,1)} %param.17) | copy-start | bytes 393220
  227.1 410.6 %copy-start.1 = (f32[1,2,1024]{2,1,0:T(2,128)S(1)}, f32[1,2,1024]{2,1,0:T(2,128)}, u32[]{:S(2)}) copy-start(f32[1,2,1024]{2,1,0:T(2,128)} %param.18) | copy-start | bytes 24580
  227.1 5.3 collective-permute-start
  241.3 5.6 collective-permute-start
  255.1 5.6 collective-permute-start
  268.9 6.6 collective-permute-start
  283.5 7.1 collective-permute-start
  298.5 7.1 collective-permute-start
  313.5 7.1 collective-permute-start
  328.5 7.1 collective-permute-start
  343.6 7.1 collective-permute-start
  358.6 7.3 collective-permute-start
  373.8 9.5 %collective-permute-start = (bf16[32,1024]{1,0:T(8,128)(2,1)}, bf16[32,1024]{1,0:T(8,128)(2,1)S(1)}, u32[]{:S(2)}, u32[]{:S(2)}) collective-permute-start(bf16[32,1024]{1,0:T(8,128)(2,1)} %get-tuple-element.309), channel_id=1, source_target_pairs={{32,0},{64,32},{96,64},{128,96},{160,128},{192,160},{224,192},{256... | collective-permute-start | bytes 196616 | tf_op jit(solution)/shard_map/while/body/eval_jaxpr/ppermute | solution.py:13
  391.3 9.5 %collective-permute-start = (bf16[32,1024]{1,0:T(8,128)(2,1)}, bf16[32,1024]{1,0:T(8,128)(2,1)S(1)}, u32[]{:S(2)}, u32[]{:S(2)}) collective-permute-start(bf16[32,1024]{1,0:T(8,128)(2,1)} %get-tuple-element.309), channel_id=1, source_target_pairs={{32,0},{64,32},{96,64},{128,96},{160,128},{192,160},{224,192},{256... | collective-permute-start | bytes 196616 | tf_op jit(solution)/shard_map/while/body/eval_jaxpr/ppermute | solution.py:13
  408.7 9.5 %collective-permute-start = (bf16[32,1024]{1,0:T(8,128)(2,1)}, bf16[32,1024]{1,0:T(8,128)(2,1)S(1)}, u32[]{:S(2)}, u32[]{:S(2)}) collective-permute-start(bf16[32,1024]{1,0:T(8,128)(2,1)} %get-tuple-element.309), channel_id=1, source_target_pairs={{32,0},{64,32},{96,64},{128,96},{160,128},{192,160},{224,192},{256... | collective-permute-start | bytes 196616 | tf_op jit(solution)/shard_map/while/body/eval_jaxpr/ppermute | solution.py:13
  426.1 9.5 %collective-permute-start = (bf16[32,1024]{1,0:T(8,128)(2,1)}, bf16[32,1024]{1,0:T(8,128)(2,1)S(1)}, u32[]{:S(2)}, u32[]{:S(2)}) collective-permute-start(bf16[32,1024]{1,0:T(8,128)(2,1)} %get-tuple-element.309), channel_id=1, source_target_pairs={{32,0},{64,32},{96,64},{128,96},{160,128},{192,160},{224,192},{256... | collective-permute-start | bytes 196616 | tf_op jit(solution)/shard_map/while/body/eval_jaxpr/ppermute | solution.py:13
  443.5 9.5 %collective-permute-start = (bf16[32,1024]{1,0:T(8,128)(2,1)}, bf16[32,1024]{1,0:T(8,128)(2,1)S(1)}, u32[]{:S(2)}, u32[]{:S(2)}) collective-permute-start(bf16[32,1024]{1,0:T(8,128)(2,1)} %get-tuple-element.309), channel_id=1, source_target_pairs={{32,0},{64,32},{96,64},{128,96},{160,128},{192,160},{224,192},{256... | collective-permute-start | bytes 196616 | tf_op jit(solution)/shard_map/while/body/eval_jaxpr/ppermute | solution.py:13
  460.9 62.9 %collective-permute-start = (bf16[32,1024]{1,0:T(8,128)(2,1)}, bf16[32,1024]{1,0:T(8,128)(2,1)S(1)}, u32[]{:S(2)}, u32[]{:S(2)}) collective-permute-start(bf16[32,1024]{1,0:T(8,128)(2,1)} %get-tuple-element.309), channel_id=1, source_target_pairs={{32,0},{64,32},{96,64},{128,96},{160,128},{192,160},{224,192},{256... | collective-permute-start | bytes 196616 | tf_op jit(solution)/shard_map/while/body/eval_jaxpr/ppermute | solution.py:13
  537.6 9.6 %collective-permute-start = (bf16[32,1024]{1,0:T(8,128)(2,1)}, bf16[32,1024]{1,0:T(8,128)(2,1)S(1)}, u32[]{:S(2)}, u32[]{:S(2)}) collective-permute-start(bf16[32,1024]{1,0:T(8,128)(2,1)} %get-tuple-element.309), channel_id=1, source_target_pairs={{32,0},{64,32},{96,64},{128,96},{160,128},{192,160},{224,192},{256... | collective-permute-start | bytes 196616 | tf_op jit(solution)/shard_map/while/body/eval_jaxpr/ppermute | solution.py:13
  561.0 9.6 %collective-permute-start = (bf16[32,1024]{1,0:T(8,128)(2,1)}, bf16[32,1024]{1,0:T(8,128)(2,1)S(1)}, u32[]{:S(2)}, u32[]{:S(2)}) collective-permute-start(bf16[32,1024]{1,0:T(8,128)(2,1)} %get-tuple-element.309), channel_id=1, source_target_pairs={{32,0},{64,32},{96,64},{128,96},{160,128},{192,160},{224,192},{256... | collective-permute-start | bytes 196616 | tf_op jit(solution)/shard_map/while/body/eval_jaxpr/ppermute | solution.py:13
  584.4 9.6 %collective-permute-start = (bf16[32,1024]{1,0:T(8,128)(2,1)}, bf16[32,1024]{1,0:T(8,128)(2,1)S(1)}, u32[]{:S(2)}, u32[]{:S(2)}) collective-permute-start(bf16[32,1024]{1,0:T(8,128)(2,1)} %get-tuple-element.309), channel_id=1, source_target_pairs={{32,0},{64,32},{96,64},{128,96},{160,128},{192,160},{224,192},{256... | collective-permute-start | bytes 196616 | tf_op jit(solution)/shard_map/while/body/eval_jaxpr/ppermute | solution.py:13
  619.3 122.4 %copy-start.4 = (f32[1,4,1024]{2,1,0:T(4,128)}, f32[1,4,1024]{2,1,0:T(4,128)S(1)}, u32[]{:S(2)}) copy-start(f32[1,4,1024]{2,1,0:T(4,128)S(1)} %broadcast_in_dim_reshape.3) | copy-start | bytes 49156
